TPU v7x, 32 devices: a whole 2x2x4 slice. The times are simulated.
32 devices in a mesh: tm: 4 (over y, x), chan: 8 (over z, core).
Axes of the slice: x: 2, y: 2, z: 4, core: 2. Of those that a mesh axis runs over, the one named last changes fastest.
Arguments:
- strain: bfloat16 [256, 16384], P('chan', 'tm'), may hold values from -6 to 6
- fir_taps: bfloat16 [256, 256], P('chan'), may hold values from -0.375 to 0.375
Outputs:
- stacked: float32 [2, 256, 256, 256], P(None, 'tm', 'chan')
All inputs are finite; a program needn't handle non-finite values.
Results may differ from a plain program's by a relative error of at most 0.0062.
Values may be sent and summed in bfloat16 or wider, within the bound.
No kernel may reach another device: no remote copies, remote signals or barrier semaphores. Data moves between devices by JAX's collectives and lax.ppermute only.
A program may use at most 128 MiB of HBM per device.

v0:
```python
import math
import jax
import jax.numpy as jnp
from jax import lax
from jax.sharding import PartitionSpec as P

SEG = 512


def shifted(value, axis, by):
    size = lax.axis_size(axis)
    pairs = [(i, i + by) for i in range(size) if 0 <= i + by < size]
    return lax.ppermute(value, axis, pairs)


def make_table():
    sample_idx = jnp.arange(SEG, dtype=jnp.int32)
    bin_idx = jnp.arange(SEG // 2, dtype=jnp.int32)
    phases = sample_idx[:, None] * bin_idx[None, :] % SEG
    angles = phases.astype(jnp.float32) * (2.0 * math.pi / SEG)
    window = 0.5 - 0.5 * jnp.cos(sample_idx.astype(jnp.float32) * (2.0 * math.pi / SEG))
    cosine = window[:, None] * jnp.cos(angles)
    sine_part = -window[:, None] * jnp.sin(angles)
    return jnp.stack([cosine, sine_part], axis=1).astype(jnp.bfloat16)


def toeplitz(fir_taps):
    tap_count = fir_taps.shape[1]
    row_idx = jnp.arange(2 * tap_count, dtype=jnp.int32)[:, None]
    col_idx = jnp.arange(tap_count, dtype=jnp.int32)[None, :]
    lag_idx = col_idx + tap_count - row_idx
    valid = (lag_idx >= 0) & (lag_idx < tap_count)
    picked = jnp.take(fir_taps, jnp.clip(lag_idx, 0, tap_count - 1), axis=1)
    return jnp.where(valid[None, :, :], picked, jnp.zeros_like(picked))


def cross_block(own_bins, other_bins):
    swapped = jnp.stack([-other_bins[:, 1], other_bins[:, 0]], axis=1)
    real_part = jnp.einsum(
        "kpsi,kpsj->kij", own_bins, other_bins, preferred_element_type=jnp.float32
    )
    imag_part = jnp.einsum("kpsi,kpsj->kij", own_bins, swapped, preferred_element_type=jnp.float32)
    return jnp.stack([real_part, imag_part], axis=0)


def shards(strain, fir_taps):
    tap_count = fir_taps.shape[1]
    channels = strain.shape[0]
    previous = shifted(strain[:, -tap_count:], "tm", 1)
    extended = jnp.concatenate([previous, strain], axis=1)
    blocks = extended.reshape(channels, -1, tap_count)
    block_pairs = jnp.concatenate([blocks[:, :-1], blocks[:, 1:]], axis=2)
    filtered = jnp.einsum(
        "cbr,cri->cbi", block_pairs, toeplitz(fir_taps), preferred_element_type=jnp.float32
    )
    whitened = filtered.reshape(channels, -1).astype(jnp.bfloat16)
    segments = whitened.reshape(channels, whitened.shape[1] // SEG, SEG)
    spectra = jnp.einsum(
        "csn,npk->kpsc", segments, make_table(), preferred_element_type=jnp.float32
    ).astype(jnp.bfloat16)
    gathered = lax.all_gather(spectra, "chan", axis=3, tiled=True)
    all_bins = lax.all_to_all(gathered, "tm", split_axis=0, concat_axis=2, tiled=True)
    factor = 1.0 / (all_bins.shape[2] * SEG)
    first_col = lax.axis_index("chan") * channels
    own_bins = lax.dynamic_slice_in_dim(all_bins, first_col, channels, 3)
    result = cross_block(own_bins, all_bins) * factor
    return result


def solution(mesh):
    placed = (P("chan", "tm"), P("chan", None))
    return jax.shard_map(
        shards, mesh=mesh, in_specs=placed, out_specs=P(None, "tm", "chan", None), check_vma=False
    )
```

profile of v0, /device:TPU:0, one launch (start us, length us, event | category | flops | bytes accessed | tf_op | source)
XLA Modules:
  0.0 581.4 jit_solution(17817019750190096485)
XLA Ops:
  6.5 0.7 slice.15
  7.3 4.8 collective-permute-start
  12.2 0.1 fusion.24
  12.4 0.3 copy.28
  12.7 0.1 broadcast_clamp_fusion
  12.7 2.3 multiply_convert_fusion
  15.0 0.4 fusion.37
  15.4 0.1 copy.16
  15.5 454.0 %gather_fusion = bf16[131072,32]{1,0:T(8,128)(2,1)} fusion(bf16[32,256]{0,1:T(8,128)(2,1)S(1)} %copy.16, s32[131072]{0:T(1024)S(1)} %broadcast_clamp_fusion), kind=kCustom, calls=%fused_computation | custom fusion | bytes 17301504 | tf_op jit(solution)/shard_map/jit(_take)/gather | solution.py:33
  469.5 30.7 %copy.17 = bf16[512,256,32]{1,0,2:T(8,128)(2,1)} copy(bf16[512,256,32]{2,1,0:T(8,128)(2,1)} %bitcast.35) | data formatting | bytes 16777216 | tf_op jit(solution)/shard_map/jit(_take)/gather | solution.py:33
  500.3 0.1 reshape.212
  500.4 0.1 fusion.49
  500.6 4.7 fusion.15
  505.3 0.1 convert_element_type.45
  505.4 1.0 fusion.18
  506.4 29.6 %all-gather.2.cloned.1.call-done = bf16[256,2,8,256]{0,3,2,1:T(8,128)(2,1)} async-done(((bf16[256,2,8,32]{0,3,2,1:T(8,128)(2,1)}), bf16[256,2,8,256]{0,3,2,1:T(8,128)(2,1)}) %all-gather.2.cloned.1.call-update) | async-done | bytes 2097168 | tf_op jit(solution)/shard_map/all_gather | solution.py:61
  536.0 4.5 copy.19
  540.5 3.6 all-to-all-start
  544.1 25.5 %all-to-all-done = bf16[256,2,8,256]{3,2,1,0:T(8,128)(2,1)S(1)} async-done(((bf16[256,2,8,256]{3,2,1,0:T(8,128)(2,1)}), bf16[256,2,8,256]{3,2,1,0:T(8,128)(2,1)S(1)}, u32[]{:S(2)}, u32[]{:S(2)}) %all-to-all-start) | async-done | bytes 2097184 | tf_op jit(solution)/shard_map/all_to_all | solution.py:62
  569.6 0.3 copy.34
  569.9 0.1 slice_negate_fusion
  570.0 1.0 convolution_bitcast_fusion
  571.1 1.0 fusion.12
  572.1 2.5 maximum_multiply_fusion
  (11 shorter events, 0.1 us)
Async XLA Ops:
  6.5 8.9 %copy-start.1 = (bf16[32,256]{1,0:T(8,128)(2,1)S(1)}, bf16[32,256]{1,0:T(8,128)(2,1)}, u32[]{:S(2)}) copy-start(bf16[32,256]{1,0:T(8,128)(2,1)} %param.3) | copy-start | bytes 49156
  6.5 529.5 %all-gather.2.cloned.1.call-start = ((), (), s32[]{:S(2)}) async-start(), calls=%async_computation.1 | async-start | bytes 2359296 | tf_op jit(solution)/shard_map/all_gather | solution.py:61
  7.3 493.0 %collective-permute-start = (bf16[32,256]{1,0:T(8,128)(2,1)S(1)}, bf16[32,256]{1,0:T(8,128)(2,1)S(1)}, u32[]{:S(2)}, u32[]{:S(2)}) collective-permute-start(bf16[32,256]{1,0:T(8,128)(2,1)S(1)} %slice.15), channel_id=1, source_target_pairs={{0,8},{8,16},{16,24},{1,9},{9,17},{17,25},{2,10},{10,18},{18,26},{... | collective-permute-start | bytes 49160 | tf_op jit(solution)/shard_map/ppermute | solution.py:13
  469.5 30.7 %copy-start = (bf16[32,4096]{1,0:T(8,128)(2,1)S(1)}, bf16[32,4096]{1,0:T(8,128)(2,1)}, u32[]{:S(2)}) copy-start(bf16[32,4096]{1,0:T(8,128)(2,1)} %param.2) | copy-start | bytes 786436
  540.5 29.1 %all-to-all-start = ((bf16[256,2,8,256]{3,2,1,0:T(8,128)(2,1)}), bf16[256,2,8,256]{3,2,1,0:T(8,128)(2,1)S(1)}, u32[]{:S(2)}, u32[]{:S(2)}) async-start(bf16[256,2,8,256]{3,2,1,0:T(8,128)(2,1)} %copy.19), calls=%async_computation | async-start | bytes 4194304 | tf_op jit(solution)/shard_map/all_to_all | solution.py:62
Sparse Core Ops, SparseCore 0:
  506.5 29.4 all-gather.1
where the time goes:
time: 583 us; the launch traced here: 581 us
  local copies, waits for them, and re-layouts  491 us (84%)
  waiting for transfers between devices  55.1 us (9%)
  between operations  13.5 us (2%)
  starting transfers between devices  8.48 us (1%)
  matrix products  7.77 us (1%)
    gather x2, local copies, waits for them, and re-layouts, toeplitz(): picked = jnp.take(fir_taps, jnp.clip(lag_idx, 0, tap_count - 1), axis=1)  485 us
    all_gather x1, waiting for transfers between devices, shards(): gathered = lax.all_gather(spectra, 'chan', axis=3, tiled=True)  29.6 us
    all_to_all x1, waiting for transfers between devices, shards(): lax.all_to_all(gathered, 'tm', split_axis=0, concat_axis=2, tiled=True)  25.5 us
  transfers between devices with their start and end apart: 3, of which 2 were waited for; matrix products, arithmetic and copies ran while one was open for 84% of the time, Pallas kernels for 0%

commit v1 on v0

--- a/solution.py
+++ b/solution.py
@@ -59,7 +59,10 @@
         "csn,npk->kpsc", segments, make_table(), preferred_element_type=jnp.float32
     ).astype(jnp.bfloat16)
     gathered = lax.all_gather(spectra, "chan", axis=3, tiled=True)
-    all_bins = lax.all_to_all(gathered, "tm", split_axis=0, concat_axis=2, tiled=True)
+    all_bins = jnp.concatenate(
+        lax.all_to_all(jnp.stack(jnp.split(gathered, lax.axis_size("tm"), axis=0)), "tm", 0, 0),
+        axis=2,
+    )
     factor = 1.0 / (all_bins.shape[2] * SEG)
     first_col = lax.axis_index("chan") * channels
     own_bins = lax.dynamic_slice_in_dim(all_bins, first_col, channels, 3)

time: 583 us -> 590 us (1.012)
    another operation x0 -> x2, local copies, waits for them, and re-layouts: none -> 8.67 us  [shards(): jnp.stack(jnp.split(gathered, lax.axis_size('tm'), axis=0))]
  transfers between devices with their start and end apart: 3 -> 3, of which waited for: 2 -> 2; matrix products, arithmetic and copies ran while one was open for 84% -> 83% of each run, Pallas kernels for 0% -> 0%
where the time goes in v1:
time: 590 us; the launch traced here: 589 us
  local copies, waits for them, and re-layouts  496 us (84%)
  waiting for transfers between devices  55.1 us (9%)
  between operations  13.5 us (2%)
  starting transfers between devices  8.48 us (1%)
  other arithmetic  8.19 us (1%)
  matrix products  7.77 us (1%)
    gather x2, local copies, waits for them, and re-layouts, toeplitz(): picked = jnp.take(fir_taps, jnp.clip(lag_idx, 0, tap_count - 1), axis=1)  485 us
    all_gather x1, waiting for transfers between devices, shards(): gathered = lax.all_gather(spectra, 'chan', axis=3, tiled=True)  29.6 us
    all_to_all x1, waiting for transfers between devices, shards(): lax.all_to_all(jnp.stack(jnp.split(gathered, lax.axis_size('tm'), axis=0)...  25.5 us
  transfers between devices with their start and end apart: 3, of which 2 were waited for; matrix products, arithmetic and copies ran while one was open for 83% of the time, Pallas kernels for 0%

profile of v1, /device:TPU:0, one launch (start us, length us, event | category | flops | bytes accessed | tf_op | source)
XLA Modules:
  0.0 588.9 jit_solution(16498076237917534550)
XLA Ops:
  6.5 0.7 slice.15
  7.3 4.8 collective-permute-start
  12.2 0.1 fusion.24
  12.4 0.3 copy.23
  12.7 2.3 multiply_convert_fusion
  15.0 0.4 fusion.37
  15.4 0.8 copy.13
  16.2 454.0 %gather_fusion = bf16[131072,32]{1,0:T(8,128)(2,1)} fusion(bf16[32,256]{0,1:T(8,128)(2,1)S(1)} %copy.13, s32[131072]{0:T(1024)S(1)} %broadcast_clamp_fusion), kind=kCustom, calls=%fused_computation | custom fusion | bytes 17301504 | tf_op jit(solution)/shard_map/jit(_take)/gather | solution.py:33
  470.2 30.7 %copy.14 = bf16[512,256,32]{1,0,2:T(8,128)(2,1)} copy(bf16[512,256,32]{2,1,0:T(8,128)(2,1)} %bitcast.42) | data formatting | bytes 16777216 | tf_op jit(solution)/shard_map/jit(_take)/gather | solution.py:33
  501.0 0.1 reshape.218
  501.1 0.1 fusion.49
  501.2 4.7 fusion.15
  506.1 1.0 fusion.18
  507.1 29.6 %all-gather.2.cloned.1.call-done = bf16[256,2,8,256]{0,3,2,1:T(8,128)(2,1)} async-done(((bf16[256,2,8,32]{0,3,2,1:T(8,128)(2,1)}), bf16[256,2,8,256]{0,3,2,1:T(8,128)(2,1)}) %all-gather.2.cloned.1.call-update) | async-done | bytes 2097168 | tf_op jit(solution)/shard_map/all_gather | solution.py:61
  536.7 3.0 slice_bitcast_fusion.3
  539.7 2.6 pad_maximum_fusion
  542.3 5.6 copy.16
  547.9 3.6 all-to-all-start
  551.6 25.5 %all-to-all-done = bf16[4,64,2,8,256]{4,3,2,1,0:T(8,128)(2,1)S(1)} async-done(((bf16[4,64,2,8,256]{4,3,2,1,0:T(8,128)(2,1)}), bf16[4,64,2,8,256]{4,3,2,1,0:T(8,128)(2,1)S(1)}, u32[]{:S(2)}, u32[]{:S(2)}) %all-to-all-start) | async-done | bytes 2097184 | tf_op jit(solution)/shard_map/all_to_all | solution.py:63
  577.1 0.3 copy.29
  577.4 0.1 slice_negate_fusion
  577.5 1.0 convolution_bitcast_fusion
  578.5 1.0 fusion.12
  579.6 2.5 maximum_multiply_fusion
  (11 shorter events, 0.3 us)
Async XLA Ops:
  6.5 530.1 %all-gather.2.cloned.1.call-start = ((), (), s32[]{:S(2)}) async-start(), calls=%async_computation.1 | async-start | bytes 2359296 | tf_op jit(solution)/shard_map/all_gather | solution.py:61
  7.3 493.7 %collective-permute-start = (bf16[32,256]{1,0:T(8,128)(2,1)S(1)}, bf16[32,256]{1,0:T(8,128)(2,1)S(1)}, u32[]{:S(2)}, u32[]{:S(2)}) collective-permute-start(bf16[32,256]{1,0:T(8,128)(2,1)S(1)} %slice.15), channel_id=1, source_target_pairs={{0,8},{8,16},{16,24},{1,9},{9,17},{17,25},{2,10},{10,18},{18,26},{... | collective-permute-start | bytes 49160 | tf_op jit(solution)/shard_map/ppermute | solution.py:13
  470.2 30.7 %copy-start = (bf16[32,4096]{1,0:T(8,128)(2,1)S(1)}, bf16[32,4096]{1,0:T(8,128)(2,1)}, u32[]{:S(2)}) copy-start(bf16[32,4096]{1,0:T(8,128)(2,1)} %param.2) | copy-start | bytes 786436
  547.9 29.1 %all-to-all-start = ((bf16[4,64,2,8,256]{4,3,2,1,0:T(8,128)(2,1)}), bf16[4,64,2,8,256]{4,3,2,1,0:T(8,128)(2,1)S(1)}, u32[]{:S(2)}, u32[]{:S(2)}) async-start(bf16[4,64,2,8,256]{4,3,2,1,0:T(8,128)(2,1)} %copy.16), calls=%async_computation | async-start | bytes 4194304 | tf_op jit(solution)/shard_map/all_to_all | solution.py:63
Sparse Core Ops, SparseCore 0:
  507.2 29.4 all-gather.1
